TPU v7x, 32 devices: a whole 2x2x4 slice. The times are simulated.
32 devices in a mesh: dp: 8 (over z, core), shard: 4 (over y, x).
Axes of the slice: x: 2, y: 2, z: 4, core: 2. Of those that a mesh axis runs over, the one named last changes fastest.
Arguments:
- grad_partials: bfloat16 [8, 32, 256, 256], P('dp', 'shard'), may hold values from -8 to 8
- owners: int32 [32, 1], P('shard'), may hold values from 0 to 7; in each aligned block of 8 rows (0 to 7, 8 to 15, ...) at most 2 rows name the same one
- weight_blocks: int32 [9], replicated, may hold values from 1 to 8, 32 in all
- stats_left: float32 [8, 4, 2, 256, 256], P('dp', 'shard'), may hold values from -6 to 6
- stats_right: float32 [8, 4, 2, 256, 256], P('dp', 'shard'), may hold values from -6 to 6
- root_left: bfloat16 [8, 4, 2, 256, 256], P('dp', 'shard'), may hold values from -0.375 to 0.375
- root_right: bfloat16 [8, 4, 2, 256, 256], P('dp', 'shard'), may hold values from -0.375 to 0.375
- second_moment: float32 [8, 4, 2, 256, 256], P('dp', 'shard'), may hold values from 0.0015 to 0.6
- master: float32 [8, 4, 2, 256, 256], P('dp', 'shard'), may hold values from -6 to 6
Outputs:
- new_left: float32 [8, 4, 2, 256, 256], P('dp', 'shard')
- new_right: float32 [8, 4, 2, 256, 256], P('dp', 'shard')
- new_moment: float32 [8, 4, 2, 256, 256], P('dp', 'shard')
- new_master: float32 [8, 4, 2, 256, 256], P('dp', 'shard')
- regathered: bfloat16 [32, 256, 256], P('shard')
Inputs may be any that keep to these rules, and one draw needn't show every extreme that they name: `owners`: in each aligned block of 8 rows (one column) no dp index is named more than 2 times; some column names one exactly 2 times. `weight_blocks`: sums to 32; the largest is 8.
All inputs are finite; a program needn't handle non-finite values.
Results may differ from a plain program's by a relative error of at most 0.0047.
Values may be sent and summed in bfloat16 or wider, within the bound.
No kernel may reach another device: no remote copies, remote signals or barrier semaphores. Data moves between devices by JAX's collectives and lax.ppermute only.
A program may use at most 128 MiB of HBM per device.

v0:
```python
import jax
import jax.numpy as jnp
from jax import lax
from jax.sharding import PartitionSpec as P

BETA = 0.95
RATE = 0.3
ADAM_EPS = 1e-08
NORM_EPS = 1e-06


def local(
    grad_partials,
    owners,
    weight_blocks,
    stats_left,
    stats_right,
    root_left,
    root_right,
    second_moment,
    master,
):
    replica = lax.axis_index("dp")
    column = lax.axis_index("shard")
    replicas = lax.axis_size("dp")
    local_grads = grad_partials[0]
    column_blocks = local_grads.shape[0]
    slot_count = stats_left.shape[2]
    owner_of = owners[:, 0]
    onehot = (owner_of[:, None] == jnp.arange(replicas, dtype=jnp.int32)[None, :]).astype(jnp.int32)
    slot_rank = jnp.sum((jnp.cumsum(onehot, axis=0) - onehot) * onehot, axis=1)
    matches = (owner_of[None, None, :] == jnp.arange(replicas, dtype=jnp.int32)[:, None, None]) & (
        slot_rank[None, None, :] == jnp.arange(slot_count, dtype=jnp.int32)[None, :, None]
    )
    slot_table = jnp.sum(
        matches.astype(jnp.int32) * jnp.arange(column_blocks, dtype=jnp.int32)[None, None, :],
        axis=2,
    )
    slot_live = jnp.any(matches, axis=2)
    my_table = lax.dynamic_index_in_dim(slot_table, replica, 0, keepdims=False)
    my_live = lax.dynamic_index_in_dim(slot_live, replica, 0, keepdims=False)
    live_float = my_live.astype(jnp.float32)[:, None, None]
    summed = lax.psum(local_grads.astype(jnp.float32), "dp")
    owned_grad = jnp.take(summed, my_table, axis=0) * live_float
    left = stats_left[0, 0]
    right = stats_right[0, 0]
    moment = second_moment[0, 0]
    weights = master[0, 0]
    global_block = column * column_blocks + my_table
    ends = jnp.cumsum(weight_blocks)
    weight_id = jnp.sum((global_block[:, None] >= ends[None, :]).astype(jnp.int32), axis=1)
    member = (
        weight_id[:, None] == jnp.arange(weight_blocks.shape[0], dtype=jnp.int32)[None, :]
    ).astype(jnp.float32) * my_live.astype(jnp.float32)[:, None]
    vnew = BETA * moment + (1.0 - BETA) * owned_grad * owned_grad
    adam = owned_grad / (jnp.sqrt(vnew) + ADAM_EPS)
    adam_terms = jnp.sum(member * jnp.sum(adam * adam, axis=(1, 2))[:, None], axis=0)
    norm_adam = lax.psum(adam_terms, ("dp", "shard"))
    highest = lax.Precision.HIGHEST
    lnew = BETA * left + (1.0 - BETA) * jnp.einsum(
        "sij,skj->sik", owned_grad, owned_grad, precision=highest
    )
    rnew = BETA * right + (1.0 - BETA) * jnp.einsum(
        "sji,sjk->sik", owned_grad, owned_grad, precision=highest
    )
    grad_half = owned_grad.astype(jnp.bfloat16)
    inner = jnp.einsum(
        "sij,sjk->sik", root_left[0, 0], grad_half, preferred_element_type=jnp.float32
    ).astype(jnp.bfloat16)
    precond = jnp.einsum(
        "sij,sjk->sik", inner, root_right[0, 0], preferred_element_type=jnp.float32
    )
    prec_terms = jnp.sum(member * jnp.sum(precond * precond, axis=(1, 2))[:, None], axis=0)
    norm_prec = lax.psum(prec_terms, ("dp", "shard"))
    scales = jnp.sqrt(norm_adam / (norm_prec + NORM_EPS))
    slot_scale = jnp.sum(member * scales[None, :], axis=1)
    wnew = weights - RATE * slot_scale[:, None, None] * precond
    live_mask = my_live[:, None, None]
    out_left = jnp.where(live_mask, lnew, left)
    out_right = jnp.where(live_mask, rnew, right)
    out_moment = jnp.where(live_mask, vnew, moment)
    out_master = jnp.where(live_mask, wnew, weights)
    gathered = lax.all_gather(out_master.astype(jnp.bfloat16), "dp", axis=0, tiled=True)
    regathered = jnp.take(gathered, owner_of * slot_count + slot_rank, axis=0)
    return (
        out_left[None, None],
        out_right[None, None],
        out_moment[None, None],
        out_master[None, None],
        regathered,
    )


def solution(mesh):
    in_specs = (
        P("dp", "shard", None, None),
        P("shard", None),
        P(),
        P("dp", "shard", None, None, None),
        P("dp", "shard", None, None, None),
        P("dp", "shard", None, None, None),
        P("dp", "shard", None, None, None),
        P("dp", "shard", None, None, None),
        P("dp", "shard", None, None, None),
    )
    out_specs = (
        P("dp", "shard", None, None, None),
        P("dp", "shard", None, None, None),
        P("dp", "shard", None, None, None),
        P("dp", "shard", None, None, None),
        P("shard", None, None),
    )
    return jax.shard_map(local, mesh=mesh, in_specs=in_specs, out_specs=out_specs, check_vma=False)
```

profile of v0, /device:TPU:0, one launch (start us, length us, event | category | flops | bytes accessed | tf_op | source)
XLA Modules:
  0.0 161.0 jit_solution(1101177767100305149)
XLA Ops:
  7.2 0.0 copy-start
  7.2 0.0 copy-start.6
  7.2 0.0 copy-start.7
  7.2 0.0 all-reduce.3.cloned.1.call-start
  7.2 2.7 %bitcast_convert_fusion = f32[8,256,256]{2,1,0:T(8,128)} fusion(bf16[1,8,256,256]{3,2,1,0:T(8,128)(2,1)} %param.9), kind=kLoop, calls=%fused_computation.12 | loop fusion | flops 524288 | bytes 3145728 | tf_op jit(solution)/shard_map/convert_element_type | solution.py:43
  10.0 0.0 copy-start.1
  10.0 0.0 copy-start.5
  10.0 0.0 all-reduce.3.cloned.1.call-update
  10.0 0.0 copy-start.2
  10.0 0.0 all-gather.2.cloned.1.call-start
  10.1 0.0 copy-done.6
  10.1 0.1 iota_compare_fusion.1
  10.2 0.2 select_reduce_fusion
  10.4 0.1 and_reduce_fusion
  10.5 0.2 dynamic-slice_reduce_fusion
  10.7 0.1 fusion.34
  10.9 0.2 dynamic-slice_reduce_fusion.1
  11.1 0.0 copy-done.7
  11.1 0.2 reduce-window.8
  11.3 0.2 fusion.36
  11.5 66.6 %all-reduce.3.cloned.1.call-done = f32[8,256,256]{2,1,0:T(8,128)} async-done(((f32[8,256,256]{2,1,0:T(8,128)}), f32[8,256,256]{2,1,0:T(8,128)}) %all-reduce.3.cloned.1.call-update) | async-done | bytes 2097168 | tf_op jit(solution)/shard_map/psum | solution.py:43
  78.1 2.2 %gather_fusion = f32[2,256,256]{2,1,0:T(8,128)S(1)} fusion(f32[8,256,256]{2,1,0:T(8,128)} %all-reduce.3.cloned.1.call-done, s32[1024]{0:T(1024)S(1)} %pad_clamp_fusion.1), kind=kCustom, calls=%fused_computation | custom fusion | bytes 1048584 | tf_op jit(solution)/shard_map/jit(_take)/gather | solution.py:44
  80.2 0.0 copy-done.1
  80.2 0.5 fusion.15
  80.7 0.0 copy-done
  80.7 0.0 copy-done.5
  80.7 0.0 copy-start.3
  80.7 0.7 multiply_reduce_fusion
  81.4 0.0 copy-start.4
  81.4 0.1 multiply_reduce_fusion.2
  81.5 39.8 %all-reduce = (f32[9]{0:T(128)S(1)}, f32[9]{0:T(128)S(1)}) all-reduce(f32[9]{0:T(128)S(1)} %get-tuple-element.6, f32[9]{0:T(128)S(1)} %get-tuple-element.5), channel_id=1, replica_groups=mesh['dp'=8,'shard'=4] {'dp','shard'}, use_global_device_ids=true, to_apply=%region_9.10 | all-reduce | flops 18 | bytes 144 | tf_op jit(solution)/shard_map/psum | solution.py:58
  121.3 0.2 multiply_reduce_fusion.1
  121.5 0.0 copy-done.2
  121.5 1.0 fusion.43
  122.5 0.0 all-gather.2.cloned.1.call-update
  122.6 0.0 copy-done.3
  122.6 2.0 %fusion.2 = f32[1,1,2,256,256]{4,3,2,1,0:T(8,128)} fusion(f32[1,1,2,256,256]{4,3,2,1,0:T(8,128)S(1)} %copy-done.3, f32[2,256,256]{2,1,0:T(8,128)S(1)} %gather_fusion, f32[2]{0:T(128)S(1)} %convert_element_type.39, pred[2]{0:T(512)(128)(4,1)S(1)} %compare_and_fusion, pred[2]{0:T(512)(128)(4,1)S(1)} %dynamic-slice_reduce_fusion), kind=kOutput, calls=%fused_computation.5 | convolution fusion | flops 403439616 | bytes 1572876 | tf_op jit(solution)/shard_map/sji,sjk->sik/dot_general | solution.py:63
  124.6 0.0 copy-done.4
  124.6 1.7 %fusion.5 = f32[1,1,2,256,256]{4,3,2,1,0:T(8,128)} fusion(f32[1,1,2,256,256]{4,3,2,1,0:T(8,128)S(1)} %copy-done.4, f32[2,256,256]{2,1,0:T(8,128)S(1)} %gather_fusion, f32[2]{0:T(128)S(1)} %convert_element_type.39, pred[2]{0:T(512)(128)(4,1)S(1)} %compare_and_fusion, pred[2]{0:T(512)(128)(4,1)S(1)} %dynamic-slice_reduce_fusion), kind=kOutput, calls=%fused_computation.9 | convolution fusion | flops 403439616 | bytes 1572876 | tf_op jit(solution)/shard_map/sij,skj->sik/dot_general | solution.py:60
  126.2 1.0 fusion.8
  127.2 23.6 %all-gather.2.cloned.1.call-done = bf16[16,256,256]{2,1,0:T(8,128)(2,1)} async-done(((bf16[2,256,256]{2,1,0:T(8,128)(2,1)}), bf16[16,256,256]{2,1,0:T(8,128)(2,1)}) %all-gather.2.cloned.1.call-update) | async-done | bytes 2097168 | tf_op jit(solution)/shard_map/all_gather | solution.py:83
  150.9 2.2 %gather_fusion.1 = bf16[8,256,256]{2,1,0:T(8,128)(2,1)S(1)} fusion(bf16[16,256,256]{2,1,0:T(8,128)(2,1)} %all-gather.2.cloned.1.call-done, s32[1024]{0:T(1024)S(1)} %pad_clamp_fusion), kind=kCustom, calls=%fused_computation.1 | custom fusion | bytes 2097184 | tf_op jit(solution)/shard_map/jit(_take)/gather | solution.py:84
  153.1 1.1 broadcast_select_fusion
  (11 shorter events, 0.1 us)
Async XLA Ops:
  7.2 73.6 %copy-start = (bf16[1,1,2,256,256]{4,3,2,1,0:T(8,128)(2,1)S(1)}, bf16[1,1,2,256,256]{4,3,2,1,0:T(8,128)(2,1)}, u32[]{:S(2)}) copy-start(bf16[1,1,2,256,256]{4,3,2,1,0:T(8,128)(2,1)} %param.15) | copy-start | bytes 786436
  7.2 2.9 %copy-start.6 = (s32[8,1]{0,1:T(1,128)S(1)}, s32[8,1]{0,1:T(1,128)}, u32[]{:S(2)}) copy-start(s32[8,1]{0,1:T(1,128)} %param.10) | copy-start | bytes 100
  7.2 3.9 %copy-start.7 = (s32[9]{0:T(128)S(1)}, s32[9]{0:T(128)}, u32[]{:S(2)}) copy-start(s32[9]{0:T(128)} %param.11) | copy-start | bytes 112
  7.2 70.9 %all-reduce.3.cloned.1.call-start = ((), (), s32[]{:S(2)}) async-start(), calls=%async_computation | async-start | bytes 4194304 | tf_op jit(solution)/shard_map/psum | solution.py:43
  10.0 70.2 %copy-start.1 = (f32[1,1,2,256,256]{4,3,2,1,0:T(8,128)S(1)}, f32[1,1,2,256,256]{4,3,2,1,0:T(8,128)}, u32[]{:S(2)}) copy-start(f32[1,1,2,256,256]{4,3,2,1,0:T(8,128)} %param.16) | copy-start | bytes 1572868
  10.0 70.7 %copy-start.5 = (bf16[1,1,2,256,256]{4,3,2,1,0:T(8,128)(2,1)S(1)}, bf16[1,1,2,256,256]{4,3,2,1,0:T(8,128)(2,1)}, u32[]{:S(2)}) copy-start(bf16[1,1,2,256,256]{4,3,2,1,0:T(8,128)(2,1)} %param.14) | copy-start | bytes 786436
  10.0 111.5 %copy-start.2 = (f32[1,1,2,256,256]{4,3,2,1,0:T(8,128)S(1)}, f32[1,1,2,256,256]{4,3,2,1,0:T(8,128)}, u32[]{:S(2)}) copy-start(f32[1,1,2,256,256]{4,3,2,1,0:T(8,128)} %param.17) | copy-start | bytes 1572868
  10.0 140.8 %all-gather.2.cloned.1.call-start = ((), (), s32[]{:S(2)}) async-start(), calls=%async_computation.1 | async-start | bytes 2359296 | tf_op jit(solution)/shard_map/all_gather | solution.py:83
  80.7 41.9 %copy-start.3 = (f32[1,1,2,256,256]{4,3,2,1,0:T(8,128)S(1)}, f32[1,1,2,256,256]{4,3,2,1,0:T(8,128)}, u32[]{:S(2)}) copy-start(f32[1,1,2,256,256]{4,3,2,1,0:T(8,128)} %param.13) | copy-start | bytes 1572868
  81.4 43.2 %copy-start.4 = (f32[1,1,2,256,256]{4,3,2,1,0:T(8,128)S(1)}, f32[1,1,2,256,256]{4,3,2,1,0:T(8,128)}, u32[]{:S(2)}) copy-start(f32[1,1,2,256,256]{4,3,2,1,0:T(8,128)} %param.12) | copy-start | bytes 1572868
Sparse Core Ops, SparseCore 0:
  10.4 67.6 all-reduce.2
  122.7 28.1 all-gather.1
where the time goes:
time: 161 us
  waiting for transfers between devices  90.2 us (56%)
  blocking collectives  39.8 us (25%)
  between operations  14.2 us (9%)
  other arithmetic  7.65 us (5%)
  local copies, waits for them, and re-layouts  4.78 us (3%)
  matrix products  4.3 us (3%)
    psum x1, waiting for transfers between devices, local(): summed = lax.psum(local_grads.astype(jnp.float32), 'dp')  66.6 us
    psum x1, blocking collectives, local(): norm_adam = lax.psum(adam_terms, ('dp', 'shard'))  39.8 us
    all_gather x1, waiting for transfers between devices, local(): lax.all_gather(out_master.astype(jnp.bfloat16), 'dp', axis=0, tiled=True)  23.6 us
  transfers between devices with their start and end apart: 2, of which 2 were waited for; matrix products, arithmetic and copies ran while one was open for 4% of the time, Pallas kernels for 0%

commit v1 on v0

--- a/solution.py
+++ b/solution.py
@@ -55,7 +55,7 @@
     vnew = BETA * moment + (1.0 - BETA) * owned_grad * owned_grad
     adam = owned_grad / (jnp.sqrt(vnew) + ADAM_EPS)
     adam_terms = jnp.sum(member * jnp.sum(adam * adam, axis=(1, 2))[:, None], axis=0)
-    norm_adam = lax.psum(adam_terms, ("dp", "shard"))
+    norm_adam = lax.psum(lax.psum(adam_terms, "shard"), "dp")
     highest = lax.Precision.HIGHEST
     lnew = BETA * left + (1.0 - BETA) * jnp.einsum(
         "sij,skj->sik", owned_grad, owned_grad, precision=highest

time: 161 us -> 183 us (1.14)
  blocking collectives: 39.8 us -> 60.4 us
    psum x1 -> x3, blocking collectives: 39.8 us -> 60.4 us  [the longest x1 36.9 us: local(): norm_prec = lax.psum(prec_terms, ('dp', 'shard'))]
  transfers between devices with their start and end apart: 2 -> 2, of which waited for: 2 -> 2; matrix products, arithmetic and copies ran while one was open for 4% -> 3% of each run, Pallas kernels for 0% -> 0%
where the time goes in v1:
time: 183 us
  waiting for transfers between devices  91.7 us (50%)
  blocking collectives  60.4 us (33%)
  between operations  14.2 us (8%)
  other arithmetic  7.65 us (4%)
  local copies, waits for them, and re-layouts  4.78 us (3%)
  matrix products  4.3 us (2%)
    psum x1, waiting for transfers between devices, local(): summed = lax.psum(local_grads.astype(jnp.float32), 'dp')  66.6 us
    psum x1, blocking collectives, local(): norm_prec = lax.psum(prec_terms, ('dp', 'shard'))  36.9 us
    all_gather x1, waiting for transfers between devices, local(): lax.all_gather(out_master.astype(jnp.bfloat16), 'dp', axis=0, tiled=True)  25.1 us
    psum x2, blocking collectives, local(): norm_adam = lax.psum(lax.psum(adam_terms, 'shard'), 'dp')  23.5 us
  transfers between devices with their start and end apart: 2, of which 2 were waited for; matrix products, arithmetic and copies ran while one was open for 3% of the time, Pallas kernels for 0%

profile of v1, /device:TPU:0, one launch (start us, length us, event | category | flops | bytes accessed | tf_op | source)
XLA Modules:
  0.0 183.1 jit_solution(7444548938891755676)
XLA Ops:
  7.2 0.0 copy-start
  7.2 0.0 copy-start.6
  7.2 0.0 copy-start.7
  7.2 0.0 all-reduce.2.cloned.1.call-start
  7.2 2.7 %bitcast_convert_fusion = f32[8,256,256]{2,1,0:T(8,128)} fusion(bf16[1,8,256,256]{3,2,1,0:T(8,128)(2,1)} %param.9), kind=kLoop, calls=%fused_computation.12 | loop fusion | flops 524288 | bytes 3145728 | tf_op jit(solution)/shard_map/convert_element_type | solution.py:43
  10.0 0.0 copy-start.1
  10.0 0.0 copy-start.5
  10.0 0.0 all-reduce.2.cloned.1.call-update
  10.0 0.0 copy-start.2
  10.0 0.0 all-gather.2.cloned.1.call-start
  10.1 0.0 copy-done.6
  10.1 0.1 iota_compare_fusion.1
  10.2 0.2 select_reduce_fusion
  10.4 0.1 and_reduce_fusion
  10.5 0.2 dynamic-slice_reduce_fusion
  10.7 0.1 fusion.34
  10.9 0.2 dynamic-slice_reduce_fusion.1
  11.1 0.0 copy-done.7
  11.1 0.2 reduce-window.8
  11.3 0.2 fusion.36
  11.5 66.6 %all-reduce.2.cloned.1.call-done = f32[8,256,256]{2,1,0:T(8,128)} async-done(((f32[8,256,256]{2,1,0:T(8,128)}), f32[8,256,256]{2,1,0:T(8,128)}) %all-reduce.2.cloned.1.call-update) | async-done | bytes 2097168 | tf_op jit(solution)/shard_map/psum | solution.py:43
  78.1 2.2 %gather_fusion = f32[2,256,256]{2,1,0:T(8,128)S(1)} fusion(f32[8,256,256]{2,1,0:T(8,128)} %all-reduce.2.cloned.1.call-done, s32[1024]{0:T(1024)S(1)} %pad_clamp_fusion.1), kind=kCustom, calls=%fused_computation | custom fusion | bytes 1048584 | tf_op jit(solution)/shard_map/jit(_take)/gather | solution.py:44
  80.2 0.0 copy-done.1
  80.2 0.5 fusion.15
  80.7 0.0 copy-done
  80.7 0.0 copy-done.5
  80.7 0.0 copy-start.3
  80.7 0.7 multiply_reduce_fusion
  81.4 0.0 copy-start.4
  81.4 0.1 multiply_reduce_fusion.2
  81.5 10.0 %psum.29 = f32[9]{0:T(128)S(1)} all-reduce(f32[9]{0:T(128)S(1)} %get-tuple-element.6), channel_id=1, replica_groups=mesh['dp'=8,'shard'=4] {'shard'}, use_global_device_ids=true, to_apply=%region_9.10 | all-reduce | flops 9 | bytes 72 | tf_op jit(solution)/shard_map/psum | solution.py:58
  91.5 13.6 %psum.30 = f32[9]{0:T(128)S(1)} all-reduce(f32[9]{0:T(128)S(1)} %psum.29), channel_id=1, replica_groups=mesh['dp'=8,'shard'=4] {'dp'}, use_global_device_ids=true, to_apply=%region_10.11 | all-reduce | flops 9 | bytes 72 | tf_op jit(solution)/shard_map/psum | solution.py:58
  105.0 36.9 %psum.31 = f32[9]{0:T(128)S(1)} all-reduce(f32[9]{0:T(128)S(1)} %get-tuple-element.5), channel_id=1, replica_groups=mesh['dp'=8,'shard'=4] {'dp','shard'}, use_global_device_ids=true, to_apply=%region_13.14 | all-reduce | flops 9 | bytes 72 | tf_op jit(solution)/shard_map/psum | solution.py:74
  141.9 0.2 multiply_reduce_fusion.1
  142.1 0.0 copy-done.2
  142.1 1.0 fusion.43
  143.2 0.0 all-gather.2.cloned.1.call-update
  143.2 0.0 copy-done.3
  143.2 2.0 %fusion.2 = f32[1,1,2,256,256]{4,3,2,1,0:T(8,128)} fusion(f32[1,1,2,256,256]{4,3,2,1,0:T(8,128)S(1)} %copy-done.3, f32[2,256,256]{2,1,0:T(8,128)S(1)} %gather_fusion, f32[2]{0:T(128)S(1)} %convert_element_type.39, pred[2]{0:T(512)(128)(4,1)S(1)} %compare_and_fusion, pred[2]{0:T(512)(128)(4,1)S(1)} %dynamic-slice_reduce_fusion), kind=kOutput, calls=%fused_computation.5 | convolution fusion | flops 403439616 | bytes 1572876 | tf_op jit(solution)/shard_map/sji,sjk->sik/dot_general | solution.py:63
  145.2 0.0 copy-done.4
  145.2 1.7 fusion.5
  146.9 1.0 fusion.8
  147.8 25.1 %all-gather.2.cloned.1.call-done = bf16[16,256,256]{2,1,0:T(8,128)(2,1)} async-done(((bf16[2,256,256]{2,1,0:T(8,128)(2,1)}), bf16[16,256,256]{2,1,0:T(8,128)(2,1)}) %all-gather.2.cloned.1.call-update) | async-done | bytes 2097168 | tf_op jit(solution)/shard_map/all_gather | solution.py:83
  172.9 2.2 %gather_fusion.1 = bf16[8,256,256]{2,1,0:T(8,128)(2,1)S(1)} fusion(bf16[16,256,256]{2,1,0:T(8,128)(2,1)} %all-gather.2.cloned.1.call-done, s32[1024]{0:T(1024)S(1)} %pad_clamp_fusion), kind=kCustom, calls=%fused_computation.1 | custom fusion | bytes 2097184 | tf_op jit(solution)/shard_map/jit(_take)/gather | solution.py:84
  175.1 1.1 broadcast_select_fusion
  (11 shorter events, 0.1 us)
Async XLA Ops:
  7.2 73.6 %copy-start = (bf16[1,1,2,256,256]{4,3,2,1,0:T(8,128)(2,1)S(1)}, bf16[1,1,2,256,256]{4,3,2,1,0:T(8,128)(2,1)}, u32[]{:S(2)}) copy-start(bf16[1,1,2,256,256]{4,3,2,1,0:T(8,128)(2,1)} %param.15) | copy-start | bytes 786436
  7.2 2.9 %copy-start.6 = (s32[8,1]{0,1:T(1,128)S(1)}, s32[8,1]{0,1:T(1,128)}, u32[]{:S(2)}) copy-start(s32[8,1]{0,1:T(1,128)} %param.10) | copy-start | bytes 100
  7.2 3.9 %copy-start.7 = (s32[9]{0:T(128)S(1)}, s32[9]{0:T(128)}, u32[]{:S(2)}) copy-start(s32[9]{0:T(128)} %param.11) | copy-start | bytes 112
  7.2 70.9 %all-reduce.2.cloned.1.call-start = ((), (), s32[]{:S(2)}) async-start(), calls=%async_computation | async-start | bytes 4194304 | tf_op jit(solution)/shard_map/psum | solution.py:43
  10.0 70.2 %copy-start.1 = (f32[1,1,2,256,256]{4,3,2,1,0:T(8,128)S(1)}, f32[1,1,2,256,256]{4,3,2,1,0:T(8,128)}, u32[]{:S(2)}) copy-start(f32[1,1,2,256,256]{4,3,2,1,0:T(8,128)} %param.16) | copy-start | bytes 1572868
  10.0 70.7 %copy-start.5 = (bf16[1,1,2,256,256]{4,3,2,1,0:T(8,128)(2,1)S(1)}, bf16[1,1,2,256,256]{4,3,2,1,0:T(8,128)(2,1)}, u32[]{:S(2)}) copy-start(bf16[1,1,2,256,256]{4,3,2,1,0:T(8,128)(2,1)} %param.14) | copy-start | bytes 786436
  10.0 132.1 %copy-start.2 = (f32[1,1,2,256,256]{4,3,2,1,0:T(8,128)S(1)}, f32[1,1,2,256,256]{4,3,2,1,0:T(8,128)}, u32[]{:S(2)}) copy-start(f32[1,1,2,256,256]{4,3,2,1,0:T(8,128)} %param.17) | copy-start | bytes 1572868
  10.0 162.9 %all-gather.2.cloned.1.call-start = ((), (), s32[]{:S(2)}) async-start(), calls=%async_computation.1 | async-start | bytes 2359296 | tf_op jit(solution)/shard_map/all_gather | solution.py:83
  80.7 62.5 %copy-start.3 = (f32[1,1,2,256,256]{4,3,2,1,0:T(8,128)S(1)}, f32[1,1,2,256,256]{4,3,2,1,0:T(8,128)}, u32[]{:S(2)}) copy-start(f32[1,1,2,256,256]{4,3,2,1,0:T(8,128)} %param.13) | copy-start | bytes 1572868
  81.4 63.8 %copy-start.4 = (f32[1,1,2,256,256]{4,3,2,1,0:T(8,128)S(1)}, f32[1,1,2,256,256]{4,3,2,1,0:T(8,128)}, u32[]{:S(2)}) copy-start(f32[1,1,2,256,256]{4,3,2,1,0:T(8,128)} %param.12) | copy-start | bytes 1572868
Sparse Core Ops, SparseCore 0:
  10.4 67.6 all-reduce.1
  143.3 29.5 all-gather.1
